TPU v7x, 32 devices: a whole 2x2x4 slice. The times are simulated.
32 devices in a mesh: space: 8 (over y, x, core), species: 4 (over z).
Axes of the slice: x: 2, y: 2, z: 4, core: 2. Of those that a mesh axis runs over, the one named last changes fastest.
Arguments:
- cotangent: bfloat16 [4, 400, 20, 1024], P('species', None, None, 'space'), may hold values from -6 to 6
- freq: float32 [4], P('species'), may hold values from 0.2 to 0.9
- ratio: float32 [4], P('species'), may hold values from 0.5 to 1
- coupling: float32 [4, 4, 13], replicated, may hold values from 0.1 to 0.6
- wall: int32 [1024], P('space'), may hold values 0 or 1
- inlet: int32 [1024], P('space'), may hold values 0 or 1
- face_type: int32 [2, 8], P(None, 'space'), may hold values from 0 to 1
Outputs:
- grad_state: bfloat16 [4, 400, 20, 1024], P('species', None, None, 'space')
Inputs may be any that keep to these rules, and one draw needn't show every extreme that they name: `wall`: 1 marks a solid cell. `inlet`: 1 marks an inlet cell. `face_type`: 0 is a specular wall, 1 a reversing wall.
All inputs are finite; a program needn't handle non-finite values. No bound on the sum of `wall` or of `inlet` on one device may be relied on, other than what follows from the above.
Results may differ from a plain program's by a relative error of at most 0.0049.
Values may be sent and summed in bfloat16 or wider, within the bound.
No kernel may reach another device: no remote copies, remote signals or barrier semaphores. Data moves between devices by JAX's collectives and lax.ppermute only.
A program may use at most 64 MiB of HBM per device.

v0:
```python
import math
import jax
import jax.numpy as jnp
from jax import lax
from jax.sharding import PartitionSpec as P

NZ = 128
courant_max = 0.45
node_reach = 2.85


def passed_along(value, axis, steps):
    count = lax.axis_size(axis)
    pairs = [(source, (source + steps) % count) for source in range(count)]
    return lax.ppermute(value, axis, pairs)


def velocity_tables(node_count):
    pair_count = node_count * node_count
    spacing = 2.0 * node_reach / (node_count - 1)
    node_line = (
        jnp.arange(node_count, dtype=jnp.int32).astype(jnp.float32) - 0.5 * (node_count - 1)
    ) * spacing
    grid_shape = (pair_count, node_count)
    along_x = jnp.broadcast_to(jnp.repeat(node_line, node_count)[:, None], grid_shape)
    along_y = jnp.broadcast_to(jnp.tile(node_line, node_count)[:, None], grid_shape)
    along_z = jnp.broadcast_to(node_line[None, :], grid_shape)
    square = along_x * along_x + along_y * along_y + along_z * along_z
    heat_term = square - 2.5
    functions = [
        jnp.ones(grid_shape, jnp.float32),
        along_x,
        along_y,
        along_z,
        square - 1.5,
        along_x * along_y,
        along_x * along_z,
        along_y * along_z,
        along_x * along_x - along_y * along_y,
        along_y * along_y - along_z * along_z,
        along_x * heat_term,
        along_y * heat_term,
        along_z * heat_term,
    ]
    stacked = jnp.stack(functions).reshape(len(functions), pair_count * node_count)
    basis_table = stacked / jnp.sqrt(jnp.mean(stacked * stacked, axis=1, keepdims=True))
    weights = jnp.exp(-square).reshape(-1) * (spacing * spacing * spacing) / math.pi**1.5
    recon_table = basis_table * weights[None, :]
    return (node_line, basis_table, recon_table)


def keep_factor(wall, inlet, pair_count):
    upward = (jnp.arange(pair_count, dtype=jnp.int32) >= pair_count // 2).astype(jnp.float32)
    open_cells = (1 - wall).astype(jnp.float32)
    inflow = inlet.astype(jnp.float32)
    return open_cells[None, None, :] * (1.0 - upward[:, None, None] * inflow[None, None, :])


def on_device(cotangent, freq, ratio, coupling, wall, inlet, face_type):
    pair_count = cotangent.shape[1]
    node_count = cotangent.shape[2]
    cell_count = cotangent.shape[3]
    depth_cells = NZ
    column_count = cell_count // depth_cells
    half_pairs = pair_count // 2
    node_line, basis_table, recon_table = velocity_tables(node_count)
    keep_mask = keep_factor(wall, inlet, pair_count)
    masked = cotangent[0] * keep_mask.astype(jnp.bfloat16)
    moments = jnp.dot(
        basis_table,
        masked.reshape(pair_count * node_count, cell_count),
        precision=lax.Precision.HIGHEST,
        preferred_element_type=jnp.float32,
    )
    species_index = lax.axis_index("species")
    rate_value = freq[0]
    row_k = lax.dynamic_index_in_dim(coupling, species_index, axis=0, keepdims=False)
    cross_terms = jnp.sum(
        row_k[:, :, None] * lax.all_gather(moments[None], "species", axis=0, tiled=True), axis=0
    )
    rebuilt = jnp.dot(
        recon_table.T,
        cross_terms,
        precision=lax.Precision.HIGHEST,
        preferred_element_type=jnp.float32,
    ).reshape(pair_count, node_count, cell_count)
    relaxed = ((1.0 - rate_value) * masked.astype(jnp.float32) + rebuilt).astype(jnp.bfloat16)
    rim_shape = (half_pairs, node_count, depth_cells)
    zero_half = jnp.zeros(rim_shape, jnp.bfloat16)
    first_upper = relaxed[half_pairs:, :, :depth_cells].reshape(
        half_pairs, node_count * depth_cells
    )
    got_next = passed_along(first_upper, "space", -1).reshape(rim_shape)
    last_lower = relaxed[:half_pairs, :, cell_count - depth_cells :].reshape(
        half_pairs, node_count * depth_cells
    )
    got_prev = passed_along(last_lower, "space", 1).reshape(rim_shape)
    next_rim = jnp.concatenate([zero_half, got_next], axis=0)
    prev_rim = jnp.concatenate([got_prev, zero_half], axis=0)
    field = relaxed.astype(jnp.float32).reshape(pair_count, node_count, column_count, depth_cells)
    scale_factor = courant_max * ratio[0] / node_reach
    adv_x = (scale_factor * jnp.repeat(node_line, node_count))[:, None, None, None]
    adv_z = (scale_factor * node_line)[None, :, None, None]
    plus_x = jnp.maximum(adv_x, 0.0)
    minus_x = jnp.maximum(-adv_x, 0.0)
    plus_z = jnp.maximum(adv_z, 0.0)
    minus_z = jnp.maximum(-adv_z, 0.0)
    shifted_up_x = jnp.concatenate(
        [field[:, :, 1:], next_rim.astype(jnp.float32)[:, :, None, :]], axis=2
    )
    shifted_down_x = jnp.concatenate(
        [prev_rim.astype(jnp.float32)[:, :, None, :], field[:, :, : column_count - 1]], axis=2
    )
    zero_plane = jnp.zeros_like(field[..., :1])
    upper_z = jnp.concatenate([field[..., 1:], zero_plane], axis=3)
    lower_z = jnp.concatenate([zero_plane, field[..., :-1]], axis=3)
    result = (1.0 - jnp.abs(adv_x) - jnp.abs(adv_z)) * field
    result = result + plus_x * shifted_up_x + minus_x * shifted_down_x
    result = result + plus_z * upper_z + minus_z * lower_z
    bottom_part = plus_z[..., 0] * field[..., 0]
    bottom_add = jnp.where(
        face_type[0][None, None, :] == 1,
        jnp.flip(bottom_part, axis=(0, 1)),
        jnp.flip(bottom_part, axis=1),
    )
    top_part = minus_z[..., 0] * field[..., depth_cells - 1]
    top_add = jnp.where(
        face_type[1][None, None, :] == 1,
        jnp.flip(top_part, axis=(0, 1)),
        jnp.flip(top_part, axis=1),
    )
    result = result.at[..., 0].add(bottom_add)
    result = result.at[..., depth_cells - 1].add(top_add)
    return result.reshape(pair_count, node_count, cell_count).astype(jnp.bfloat16)[None]


def solution(mesh):
    in_specs = (
        P("species", None, None, "space"),
        P("species"),
        P("species"),
        P(),
        P("space"),
        P("space"),
        P(None, "space"),
    )
    out_specs = P("species", None, None, "space")
    return jax.shard_map(
        on_device, mesh=mesh, in_specs=in_specs, out_specs=out_specs, check_vma=False
    )
```

profile of v0, /device:TPU:1, one launch (start us, length us, event | category | flops | bytes accessed | tf_op | source)
XLA Modules:
  0.0 108.2 jit_solution(7815667221158033408)
XLA Ops:
  6.1 2.8 %dot_general.11 = f32[400,20,13]{1,0,2:T(8,128)S(1)} reshape(f32[8000,13]{0,1:T(8,128)} %multiply_bitcast_fusion) | data formatting | bytes 832000 | tf_op jit(solution)/shard_map/dot_general | solution.py:81
  9.0 2.7 %copy.47 = f32[400,20,13]{0,2,1:T(8,128)} copy(f32[400,20,13]{1,0,2:T(8,128)S(1)} %dot_general.11) | data formatting | bytes 832000 | tf_op jit(solution)/shard_map/dot_general | solution.py:81
  12.4 2.2 %copy.45 = bf16[1,400,20,128]{3,2,1,0:T(8,128)(2,1)S(1)} copy(bf16[1,400,20,128]{3,1,2,0:T(8,128)(2,1)} %param.11) | data formatting | bytes 4096000 | tf_op args[0]
  14.5 2.0 %squeeze.18 = bf16[8000,128]{1,0:T(8,128)(2,1)} reshape(bf16[1,400,20,128]{3,2,1,0:T(8,128)(2,1)S(1)} %copy.45) | data formatting | bytes 4096000 | tf_op jit(solution)/shard_map/squeeze | solution.py:68
  17.0 2.0 %mul.363 = bf16[8000,128]{1,0:T(8,128)(2,1)} reshape(bf16[400,20,128]{2,1,0:T(8,128)(2,1)S(1)} %mul.346.clone) | data formatting | bytes 4096000 | tf_op jit(solution)/shard_map/mul | solution.py:68
  19.0 3.3 %fusion.8 = f32[1,13,128]{2,1,0:T(8,128)S(1)} fusion(bf16[8000,128]{1,0:T(8,128)(2,1)} %squeeze.18, bf16[8000,128]{1,0:T(8,128)(2,1)} %mul.363, f32[13,8000]{1,0:T(8,128)S(1)} %stack.24, f32[13]{0:T(128)S(1)} %multiply_sqrt_fusion), kind=kOutput, calls=%fused_computation.17 | convolution fusion | flops 160872000 | bytes 4518708 | tf_op jit(solution)/shard_map/dot_general | solution.py:69
  22.3 11.6 %all-gather.1 = f32[4,13,128]{2,1,0:T(8,128)S(1)} all-gather(f32[1,13,128]{2,1,0:T(8,128)S(1)} %fusion.8), channel_id=2, replica_groups=mesh['space'=8,'species'=4] {'species'}, dimensions={0}, use_global_device_ids=true | all-gather | bytes 33280 | tf_op jit(solution)/shard_map/all_gather | solution.py:79
  34.0 8.1 %add_convert_fusion = bf16[400,20,128]{2,0,1:T(8,128)(2,1)S(1)} fusion(f32[400,20,13]{0,2,1:T(8,128)} %copy.47, bf16[1,400,20,128]{3,1,2,0:T(8,128)(2,1)} %param.11, f32[]{:T(128)} %bitcast.2, bf16[400,128]{1,0:T(8,128)(2,1)S(1)} %multiply_convert_fusion, f32[13,128]{1,0:T(8,128)S(1)} %multiply_reduce_fusion.1), kind=kOutput, calls=%fused_computation.12 | convolution fusion | flops 164864000 | bytes 4621060 | tf_op jit(solution)/shard_map/dot_general | solution.py:81
  42.5 4.4 %collective-permute-start.1 = (bf16[200,2560]{1,0:T(8,128)(2,1)S(1)}, bf16[200,2560]{1,0:T(8,128)(2,1)}, u32[]{:S(2)}, u32[]{:S(2)}) collective-permute-start(bf16[200,2560]{1,0:T(8,128)(2,1)S(1)} %bitcast.71), channel_id=1, source_target_pairs={{0,4},{4,8},{8,12},{12,16},{16,20},{20,24},{24,28},{28,0},{1,5},{5... | collective-permute-start | bytes 3072008 | tf_op jit(solution)/shard_map/ppermute | solution.py:15
  46.9 1.1 %copy.65 = bf16[20,25,8,128]{3,2,0,1:T(8,128)(2,1)} copy(bf16[20,25,8,128]{3,2,1,0:T(8,128)(2,1)S(1)} %get-tuple-element.35) | data formatting | bytes 2048000 | tf_op jit(solution)/shard_map/reshape | solution.py:90
  49.1 3.8 %slice_reduce_fusion = (f32[400,20]{0,1:T(8,128)S(1)}, f32[400,20]{0,1:T(8,128)S(1)}) fusion(f32[400,20,1,128]{3,0,1,2:T(8,128)S(1)} %convert_bitcast_fusion), kind=kLoop, calls=%fused_computation.7 | loop fusion | bytes 128000 | tf_op jit(solution)/shard_map/slice | solution.py:126
  54.3 2.7 %copy.52 = f32[400,20,1,1]{3,0,1,2:T(8,128)} copy(f32[400,20,1,1]{0,2,1,3:T(1,128)S(1)} %fusion.11) | data formatting | bytes 64000 | tf_op jit(solution)/shard_map/reshape.57
  58.4 2.7 %copy.53 = f32[400,20,1,1]{3,0,1,2:T(8,128)} copy(f32[400,20,1,1]{0,2,1,3:T(1,128)S(1)} %fusion.12) | data formatting | bytes 64000 | tf_op jit(solution)/shard_map/reshape.68
  61.2 4.7 %fusion.22 = (f32[400,20,1,127]{3,0,1,2:T(8,128)S(1)}, f32[400,20,1,127]{3,0,1,2:T(8,128)S(1)}) fusion(f32[400,20,1,128]{3,0,1,2:T(8,128)} %copy-done.1), kind=kLoop, calls=%fused_computation.60 | loop fusion | bytes 16256000 | tf_op jit(solution)/shard_map/slice | solution.py:115
  66.3 1.4 %copy_bitcast_fusion.2 = bf16[200,20,128]{2,0,1:T(8,128)(2,1)S(1)} fusion(bf16[200,2560]{1,0:T(8,128)(2,1)} %collective-permute-done.1), kind=kLoop, calls=%fused_computation.20 | loop fusion | bytes 2048000 | tf_op jit(solution)/shard_map/reshape | solution.py:97
  67.6 3.4 %collective-permute-done = bf16[200,2560]{1,0:T(8,128)(2,1)} collective-permute-done((bf16[200,2560]{1,0:T(8,128)(2,1)}, bf16[200,2560]{1,0:T(8,128)(2,1)}, u32[]{:S(2)}, u32[]{:S(2)}) %collective-permute-start) | collective-permute-done | bytes 1024032 | tf_op jit(solution)/shard_map/ppermute | solution.py:15
  71.1 1.4 %copy_bitcast_fusion.3 = bf16[200,20,128]{2,0,1:T(8,128)(2,1)S(1)} fusion(bf16[200,2560]{1,0:T(8,128)(2,1)} %collective-permute-done), kind=kLoop, calls=%fused_computation.21 | loop fusion | bytes 2048000 | tf_op jit(solution)/shard_map/reshape | solution.py:93
  72.5 3.1 %fusion.4 = f32[400,20,1,128]{3,0,1,2:T(8,128)S(1)} fusion(bf16[400,20,128]{2,0,1:T(8,128)(2,1)S(1)} %add_convert_fusion, f32[400,20,1,127]{3,0,1,2:T(8,128)S(1)} %get-tuple-element.34, f32[400,20,1,127]{3,0,1,2:T(8,128)S(1)} %get-tuple-element.33, f32[20]{0:T(128)S(1)} %get-tuple-element.56, f32[20]{0:T(128)S(1)} %get-tuple-element.57, ...), kind=kLoop, calls=%fused_computation.6 | loop fusion | flops 12288000 | bytes 16355360 | tf_op jit(solution)/shard_map/add | solution.py:119
  75.6 1.9 %copy-done.2 = f32[400,20,1,128]{3,0,1,2:T(8,128)} copy-done((f32[400,20,1,128]{3,0,1,2:T(8,128)}, f32[400,20,1,128]{3,0,1,2:T(8,128)S(1)}, u32[]{:S(2)}) %copy-start.2) | copy-done | bytes 4096024
  77.5 2.4 %slice_add_fusion.1 = f32[400,20,1,1]{3,0,1,2:T(8,128)} fusion(f32[400,20,1,1]{3,0,1,2:T(8,128)S(1)} %copy-done.3, f32[400,20,1,128]{3,0,1,2:T(8,128)S(1)} %fusion.4), kind=kLoop, calls=%fused_computation.11 | loop fusion | flops 8000 | bytes 96000 | tf_op jit(solution)/shard_map/add | solution.py:132
  79.8 8.3 %scatter-add.6 = f32[400,20,1,128]{3,0,1,2:T(8,128)} dynamic-update-slice(f32[400,20,1,128]{3,0,1,2:T(8,128)} %copy-done.2, f32[400,20,1,1]{3,0,1,2:T(8,128)} %slice_add_fusion.1, s32[]{:T(128)} %constant.110.clone.1, s32[]{:T(128)} %constant.110.clone.1, s32[]{:T(128)} %constant.110.clone.1, s32[]{:T(128)} %constant.110.clone.1) | dynamic-update-slice | bytes 64004 | tf_op jit(solution)/shard_map/scatter-add | solution.py:132
  88.1 6.5 %fusion.5 = f32[400,20,1]{2,0,1:T(8,128)} fusion(f32[400,20,1,1]{3,0,1,2:T(8,128)} %copy.53, f32[400,20,1,128]{3,0,1,2:T(8,128)} %scatter-add.6), kind=kLoop, calls=%fused_computation.9 | loop fusion | flops 8000 | bytes 96000 | tf_op jit(solution)/shard_map/reshape | solution.py:134
  94.6 9.9 %scatter-add.9 = f32[400,20,128]{2,0,1:T(8,128)} dynamic-update-slice(f32[400,20,128]{2,0,1:T(8,128)} %bitcast.70, f32[400,20,1]{2,0,1:T(8,128)} %fusion.5, s32[]{:T(128)} %constant.110.clone.1, s32[]{:T(128)} %constant.110.clone.1, s32[]{:T(128)} %constant.114.clone.1) | dynamic-update-slice | bytes 64004 | tf_op jit(solution)/shard_map/scatter-add | solution.py:133
  104.4 3.7 %convert_bitcast_fusion.1 = bf16[1,400,20,128]{3,1,2,0:T(8,128)(2,1)} fusion(f32[400,20,128]{2,0,1:T(8,128)} %scatter-add.9), kind=kLoop, calls=%fused_computation.14 | loop fusion | flops 1024000 | bytes 6144000 | tf_op jit(solution)/shard_map/broadcast_in_dim | solution.py:134
  (71 shorter events, 9.1 us)
Async XLA Ops:
  0.0 33.9 %copy-start = (f32[4,4,13]{2,1,0:T(4,128)S(1)}, f32[4,4,13]{2,1,0:T(4,128)}, u32[]{:S(2)}) copy-start(f32[4,4,13]{2,1,0:T(4,128)} %param.14) | copy-start | bytes 2500
  5.0 7.3 %copy-start.5 = (s32[128]{0:T(128)S(1)}, s32[128]{0:T(128)}, u32[]{:S(2)}) copy-start(s32[128]{0:T(128)} %param.16) | copy-start | bytes 1540
  5.0 7.3 %copy-start.6 = (s32[128]{0:T(128)S(1)}, s32[128]{0:T(128)}, u32[]{:S(2)}) copy-start(s32[128]{0:T(128)} %param.15) | copy-start | bytes 1540
  42.5 23.8 %collective-permute-start.1 = (bf16[200,2560]{1,0:T(8,128)(2,1)S(1)}, bf16[200,2560]{1,0:T(8,128)(2,1)}, u32[]{:S(2)}, u32[]{:S(2)}) collective-permute-start(bf16[200,2560]{1,0:T(8,128)(2,1)S(1)} %bitcast.71), channel_id=1, source_target_pairs={{0,4},{4,8},{8,12},{12,16},{16,20},{20,24},{24,28},{28,0},{1,5},{5... | collective-permute-start | bytes 3072008 | tf_op jit(solution)/shard_map/ppermute | solution.py:15
  46.9 1.4 %copy-start.4 = (s32[2,1]{0,1:T(1,128)S(1)}, s32[2,1]{0,1:T(1,128)}, u32[]{:S(2)}) copy-start(s32[2,1]{0,1:T(1,128)} %param.17) | copy-start | bytes 28
  48.0 23.1 %collective-permute-start = (bf16[200,2560]{1,0:T(8,128)(2,1)}, bf16[200,2560]{1,0:T(8,128)(2,1)}, u32[]{:S(2)}, u32[]{:S(2)}) collective-permute-start(bf16[200,2560]{1,0:T(8,128)(2,1)} %bitcast.69), channel_id=1, source_target_pairs={{0,28},{4,0},{8,4},{12,8},{16,12},{20,16},{24,20},{28,24},{1,29},{... | collective-permute-start | bytes 3072008 | tf_op jit(solution)/shard_map/ppermute | solution.py:15
  48.3 4.6 %copy-start.1 = (f32[400,20,1,128]{3,0,1,2:T(8,128)}, f32[400,20,1,128]{3,0,1,2:T(8,128)S(1)}, u32[]{:S(2)}) copy-start(f32[400,20,1,128]{3,0,1,2:T(8,128)S(1)} %convert_bitcast_fusion) | copy-start | bytes 12288004
  72.5 5.0 %copy-start.3 = (f32[400,20,1,1]{3,0,1,2:T(8,128)S(1)}, f32[400,20,1,1]{3,0,1,2:T(8,128)}, u32[]{:S(2)}) copy-start(f32[400,20,1,1]{3,0,1,2:T(8,128)} %copy.52) | copy-start | bytes 96004
  75.6 1.9 %copy-start.2 = (f32[400,20,1,128]{3,0,1,2:T(8,128)}, f32[400,20,1,128]{3,0,1,2:T(8,128)S(1)}, u32[]{:S(2)}) copy-start(f32[400,20,1,128]{3,0,1,2:T(8,128)S(1)} %fusion.4) | copy-start | bytes 12288004
where the time goes:
time: 109 us; the launch traced here: 108 us
  local copies, waits for them, and re-layouts  55.8 us (51%)
  other arithmetic  18.1 us (17%)
  blocking collectives  11.6 us (11%)
  matrix products  11.4 us (10%)
  starting transfers between devices  4.42 us (4%)
  waiting for transfers between devices  3.78 us (3%)
  between operations  3.02 us (3%)
    all_gather x1, blocking collectives, on_device(): lax.all_gather(moments[None], 'species', axis=0, tiled=True)  11.6 us
    scatter-add x1, local copies, waits for them, and re-layouts, on_device(): result = result.at[..., depth_cells - 1].add(top_add)  9.88 us
    scatter-add x1, local copies, waits for them, and re-layouts, on_device(): result = result.at[..., 0].add(bottom_add)  8.28 us
    dot_general x1, matrix products, on_device(): jnp.dot(recon_table.T, cross_terms, precision=lax.Precision.HIGHEST, pref...  8.12 us
    reshape x1, other arithmetic, on_device(): result.reshape(pair_count, node_count, cell_count).astype(jnp.bfloat16)  6.46 us
    dot_general x2, local copies, waits for them, and re-layouts, on_device(): jnp.dot(recon_table.T, cross_terms, precision=lax.Precision.HIGHEST, pref...  5.52 us
    another operation x2, local copies, waits for them, and re-layouts  5.33 us
    unnamed x18, local copies, waits for them, and re-layouts  5.31 us
  transfers between devices with their start and end apart: 2, of which 2 were waited for; matrix products, arithmetic and copies ran while one was open for 18% of the time, Pallas kernels for 0%

commit v1 on v0

--- a/solution.py
+++ b/solution.py
@@ -7,6 +7,13 @@
 NZ = 128
 courant_max = 0.45
 node_reach = 2.85
+
+
+def play_islands(xs, axis_no):
+    return jnp.concatenate(
+        jax.lax.all_to_all(jnp.stack([xs] * jax.lax.axis_size("species"), 0), "species", 0, 0),
+        axis_no,
+    )
 
 
 def passed_along(value, axis, steps):
@@ -75,9 +82,7 @@
     species_index = lax.axis_index("species")
     rate_value = freq[0]
     row_k = lax.dynamic_index_in_dim(coupling, species_index, axis=0, keepdims=False)
-    cross_terms = jnp.sum(
-        row_k[:, :, None] * lax.all_gather(moments[None], "species", axis=0, tiled=True), axis=0
-    )
+    cross_terms = jnp.sum(row_k[:, :, None] * play_islands(moments[None], 0), axis=0)
     rebuilt = jnp.dot(
         recon_table.T,
         cross_terms,

time: 109 us -> 103 us (0.945)
  blocking collectives: 11.6 us -> 0 us
  starting transfers between devices: 4.42 us -> 7.52 us
  waiting for transfers between devices: 3.78 us -> 6.13 us
    all_gather x1 -> x0, blocking collectives: 11.6 us -> none  [on_device(): lax.all_gather(moments[None], 'species', axis=0, tiled=True)]
    all_to_all x0 -> x1, starting transfers between devices: none -> 5.41 us  [play_islands(): jax.lax.all_to_all(jnp.stack([xs] * jax.lax.axis_size('species'), 0), 'sp...]
    ppermute x2, waiting for transfers between devices: 3.78 us -> 6.13 us  [passed_along(): return lax.ppermute(value, axis, pairs)]
    ppermute x2, starting transfers between devices: 4.42 us -> 2.11 us  [passed_along(): return lax.ppermute(value, axis, pairs)]
    dot_general x2, local copies, waits for them, and re-layouts: 5.52 us -> 3.73 us  [on_device(): jnp.dot(recon_table.T, cross_terms, precision=lax.Precision.HIGHEST, pref...]
    unnamed x18 -> x26, local copies, waits for them, and re-layouts: 5.31 us -> 5.99 us
    another operation x2 -> x3, local copies, waits for them, and re-layouts: 5.33 us -> 5.96 us
  transfers between devices with their start and end apart: 2 -> 3, of which waited for: 2 -> 2; matrix products, arithmetic and copies ran while one was open for 18% -> 23% of each run, Pallas kernels for 0% -> 0%
where the time goes in v1:
time: 103 us
  local copies, waits for them, and re-layouts  55.3 us (54%)
  other arithmetic  19.1 us (19%)
  matrix products  11.3 us (11%)
  starting transfers between devices  7.52 us (7%)
  waiting for transfers between devices  6.13 us (6%)
  between operations  3.1 us (3%)
    scatter-add x1, local copies, waits for them, and re-layouts, on_device(): result = result.at[..., depth_cells - 1].add(top_add)  9.89 us
    scatter-add x1, local copies, waits for them, and re-layouts, on_device(): result = result.at[..., 0].add(bottom_add)  8.26 us
    dot_general x1, matrix products, on_device(): jnp.dot(recon_table.T, cross_terms, precision=lax.Precision.HIGHEST, pref...  8.03 us
    reshape x1, other arithmetic, on_device(): result.reshape(pair_count, node_count, cell_count).astype(jnp.bfloat16)  6.43 us
    ppermute x2, waiting for transfers between devices, passed_along(): return lax.ppermute(value, axis, pairs)  6.13 us
    unnamed x26, local copies, waits for them, and re-layouts  5.99 us
    all_to_all x1, starting transfers between devices, play_islands(): jax.lax.all_to_all(jnp.stack([xs] * jax.lax.axis_size('species'), 0), 'sp...  5.41 us
    another operation x2, local copies, waits for them, and re-layouts  5.33 us
  transfers between devices with their start and end apart: 3, of which 2 were waited for; matrix products, arithmetic and copies ran while one was open for 23% of the time, Pallas kernels for 0%

profile of v1, /device:TPU:1, one launch (start us, length us, event | category | flops | bytes accessed | tf_op | source)
XLA Modules:
  0.0 102.6 jit_solution(1605385045028398546)
XLA Ops:
  5.6 2.2 %copy.56 = bf16[1,400,20,128]{3,2,1,0:T(8,128)(2,1)S(1)} copy(bf16[1,400,20,128]{3,1,2,0:T(8,128)(2,1)} %param.11) | data formatting | bytes 4096000 | tf_op args[0]
  7.7 2.0 %squeeze.18 = bf16[8000,128]{1,0:T(8,128)(2,1)} reshape(bf16[1,400,20,128]{3,2,1,0:T(8,128)(2,1)S(1)} %copy.56) | data formatting | bytes 4096000 | tf_op jit(solution)/shard_map/squeeze | solution.py:75
  10.8 2.1 %mul.363 = bf16[8000,128]{1,0:T(8,128)(2,1)} reshape(bf16[400,20,128]{2,1,0:T(8,128)(2,1)S(1)} %mul.346.clone) | data formatting | bytes 4096000 | tf_op jit(solution)/shard_map/mul | solution.py:75
  12.8 3.3 %fusion.6 = f32[13,128]{1,0:T(8,128)S(1)} fusion(bf16[8000,128]{1,0:T(8,128)(2,1)} %squeeze.18, bf16[8000,128]{1,0:T(8,128)(2,1)} %mul.363, f32[13,8000]{1,0:T(8,128)S(1)} %stack.27, f32[13]{0:T(128)S(1)} %multiply_sqrt_fusion), kind=kOutput, calls=%fused_computation.15 | convolution fusion | flops 160872000 | bytes 4518708 | tf_op jit(solution)/shard_map/dot_general | solution.py:76
  16.8 5.4 %all-to-all-start = ((f32[4,1,13,128]{3,1,2,0:T(1,128)}), f32[4,1,13,128]{3,1,2,0:T(1,128)}, u32[]{:S(2)}, u32[]{:S(2)}) async-start(f32[4,1,13,128]{3,1,2,0:T(1,128)} %stack.28), calls=%async_computation | async-start | bytes 53248 | tf_op jit(solution)/shard_map/all_to_all | solution.py:14
  23.9 1.8 %dot_general.11 = f32[400,20,13]{1,0,2:T(8,128)S(1)} reshape(f32[8000,13]{0,1:T(8,128)S(1)} %multiply_bitcast_fusion) | data formatting | bytes 832000 | tf_op jit(solution)/shard_map/dot_general | solution.py:86
  25.7 2.0 %copy.59 = f32[400,20,13]{0,2,1:T(8,128)S(1)} copy(f32[400,20,13]{1,0,2:T(8,128)S(1)} %dot_general.11) | data formatting | bytes 832000 | tf_op jit(solution)/shard_map/dot_general | solution.py:86
  30.5 8.0 %add_convert_fusion = bf16[400,20,128]{2,0,1:T(8,128)(2,1)S(1)} fusion(f32[400,20,13]{0,2,1:T(8,128)S(1)} %copy.59, bf16[1,400,20,128]{3,1,2,0:T(8,128)(2,1)} %param.11, f32[]{:T(128)} %bitcast.2, bf16[400,128]{1,0:T(8,128)(2,1)} %copy-done.4, f32[13,128]{1,0:T(8,128)S(1)} %fusion.10), kind=kOutput, calls=%fused_computation.12 | convolution fusion | flops 164864000 | bytes 4621060 | tf_op jit(solution)/shard_map/dot_general | solution.py:86
  39.2 2.1 %collective-permute-start.1 = (bf16[200,2560]{1,0:T(8,128)(2,1)S(1)}, bf16[200,2560]{1,0:T(8,128)(2,1)}, u32[]{:S(2)}, u32[]{:S(2)}) collective-permute-start(bf16[200,2560]{1,0:T(8,128)(2,1)S(1)} %bitcast.73), channel_id=1, source_target_pairs={{0,4},{4,8},{8,12},{12,16},{16,20},{20,24},{24,28},{28,0},{1,5},{5... | collective-permute-start | bytes 3072008 | tf_op jit(solution)/shard_map/ppermute | solution.py:22
  42.4 3.8 %slice_reduce_fusion = (f32[400,20]{0,1:T(8,128)S(1)}, f32[400,20]{0,1:T(8,128)S(1)}) fusion(f32[400,20,1,128]{3,0,1,2:T(8,128)S(1)} %convert_bitcast_fusion), kind=kLoop, calls=%fused_computation.7 | loop fusion | bytes 128000 | tf_op jit(solution)/shard_map/slice | solution.py:131
  47.1 2.7 %copy.64 = f32[400,20,1,1]{3,0,1,2:T(8,128)} copy(f32[400,20,1,1]{0,2,1,3:T(1,128)S(1)} %fusion.8) | data formatting | bytes 64000 | tf_op jit(solution)/shard_map/reshape.58
  50.6 2.6 %copy.65 = f32[400,20,1,1]{3,0,1,2:T(8,128)} copy(f32[400,20,1,1]{0,2,1,3:T(1,128)S(1)} %fusion.9) | data formatting | bytes 64000 | tf_op jit(solution)/shard_map/reshape.69
  53.2 4.7 %fusion.20 = (f32[400,20,1,127]{3,0,1,2:T(8,128)S(1)}, f32[400,20,1,127]{3,0,1,2:T(8,128)S(1)}) fusion(f32[400,20,1,128]{3,0,1,2:T(8,128)} %copy-done.1), kind=kLoop, calls=%fused_computation.60 | loop fusion | bytes 16256000 | tf_op jit(solution)/shard_map/slice | solution.py:120
  57.9 2.7 %collective-permute-done.1 = bf16[200,2560]{1,0:T(8,128)(2,1)} collective-permute-done((bf16[200,2560]{1,0:T(8,128)(2,1)S(1)}, bf16[200,2560]{1,0:T(8,128)(2,1)}, u32[]{:S(2)}, u32[]{:S(2)}) %collective-permute-start.1) | collective-permute-done | bytes 1024032 | tf_op jit(solution)/shard_map/ppermute | solution.py:22
  60.6 1.4 %copy_bitcast_fusion.2 = bf16[200,20,128]{2,0,1:T(8,128)(2,1)S(1)} fusion(bf16[200,2560]{1,0:T(8,128)(2,1)} %collective-permute-done.1), kind=kLoop, calls=%fused_computation.19 | loop fusion | bytes 2048000 | tf_op jit(solution)/shard_map/reshape | solution.py:102
  62.0 3.4 %collective-permute-done = bf16[200,2560]{1,0:T(8,128)(2,1)} collective-permute-done((bf16[200,2560]{1,0:T(8,128)(2,1)}, bf16[200,2560]{1,0:T(8,128)(2,1)}, u32[]{:S(2)}, u32[]{:S(2)}) %collective-permute-start) | collective-permute-done | bytes 1024032 | tf_op jit(solution)/shard_map/ppermute | solution.py:22
  65.5 1.4 %copy_bitcast_fusion.3 = bf16[200,20,128]{2,0,1:T(8,128)(2,1)S(1)} fusion(bf16[200,2560]{1,0:T(8,128)(2,1)} %collective-permute-done), kind=kLoop, calls=%fused_computation.20 | loop fusion | bytes 2048000 | tf_op jit(solution)/shard_map/reshape | solution.py:98
  66.9 3.1 %fusion.4 = f32[400,20,1,128]{3,0,1,2:T(8,128)S(1)} fusion(bf16[400,20,128]{2,0,1:T(8,128)(2,1)S(1)} %add_convert_fusion, f32[400,20,1,127]{3,0,1,2:T(8,128)S(1)} %get-tuple-element.34, f32[400,20,1,127]{3,0,1,2:T(8,128)S(1)} %get-tuple-element.33, f32[20]{0:T(128)S(1)} %get-tuple-element.56, f32[20]{0:T(128)S(1)} %copy-done.7, ...), kind=kLoop, calls=%fused_computation.6 | loop fusion | flops 12288000 | bytes 16355360 | tf_op jit(solution)/shard_map/add | solution.py:124
  70.0 1.9 %copy-done.2 = f32[400,20,1,128]{3,0,1,2:T(8,128)} copy-done((f32[400,20,1,128]{3,0,1,2:T(8,128)}, f32[400,20,1,128]{3,0,1,2:T(8,128)S(1)}, u32[]{:S(2)}) %copy-start.2) | copy-done | bytes 4096024
  71.9 2.3 %slice_add_fusion.1 = f32[400,20,1,1]{3,0,1,2:T(8,128)} fusion(f32[400,20,1,1]{3,0,1,2:T(8,128)S(1)} %copy-done.3, f32[400,20,1,128]{3,0,1,2:T(8,128)S(1)} %fusion.4), kind=kLoop, calls=%fused_computation.11 | loop fusion | flops 8000 | bytes 96000 | tf_op jit(solution)/shard_map/add | solution.py:137
  74.3 8.3 %scatter-add.6 = f32[400,20,1,128]{3,0,1,2:T(8,128)} dynamic-update-slice(f32[400,20,1,128]{3,0,1,2:T(8,128)} %copy-done.2, f32[400,20,1,1]{3,0,1,2:T(8,128)} %slice_add_fusion.1, s32[]{:T(128)} %constant.110.clone.1, s32[]{:T(128)} %constant.110.clone.1, s32[]{:T(128)} %constant.110.clone.1, s32[]{:T(128)} %constant.110.clone.1) | dynamic-update-slice | bytes 64004 | tf_op jit(solution)/shard_map/scatter-add | solution.py:137
  82.5 6.4 %fusion.5 = f32[400,20,1]{2,0,1:T(8,128)} fusion(f32[400,20,1,1]{3,0,1,2:T(8,128)} %copy.65, f32[400,20,1,128]{3,0,1,2:T(8,128)} %scatter-add.6), kind=kLoop, calls=%fused_computation.9 | loop fusion | flops 8000 | bytes 96000 | tf_op jit(solution)/shard_map/reshape | solution.py:139
  89.0 9.9 %scatter-add.9 = f32[400,20,128]{2,0,1:T(8,128)} dynamic-update-slice(f32[400,20,128]{2,0,1:T(8,128)} %bitcast.72, f32[400,20,1]{2,0,1:T(8,128)} %fusion.5, s32[]{:T(128)} %constant.110.clone.1, s32[]{:T(128)} %constant.110.clone.1, s32[]{:T(128)} %constant.114.clone.1) | dynamic-update-slice | bytes 64004 | tf_op jit(solution)/shard_map/scatter-add | solution.py:138
  98.8 3.7 %convert_bitcast_fusion.1 = bf16[1,400,20,128]{3,1,2,0:T(8,128)(2,1)} fusion(f32[400,20,128]{2,0,1:T(8,128)} %scatter-add.9), kind=kLoop, calls=%fused_computation.14 | loop fusion | flops 1024000 | bytes 6144000 | tf_op jit(solution)/shard_map/broadcast_in_dim | solution.py:139
  (82 shorter events, 12.2 us)
Async XLA Ops:
  0.0 23.3 %copy-start = (f32[4,4,13]{2,1,0:T(4,128)S(1)}, f32[4,4,13]{2,1,0:T(4,128)}, u32[]{:S(2)}) copy-start(f32[4,4,13]{2,1,0:T(4,128)} %param.14) | copy-start | bytes 2500
  0.0 5.5 %copy-start.9 = (s32[128]{0:T(128)S(1)}, s32[128]{0:T(128)}, u32[]{:S(2)}) copy-start(s32[128]{0:T(128)} %param.16) | copy-start | bytes 1540
  0.0 5.5 %copy-start.10 = (s32[128]{0:T(128)S(1)}, s32[128]{0:T(128)}, u32[]{:S(2)}) copy-start(s32[128]{0:T(128)} %param.15) | copy-start | bytes 1540
  9.8 0.6 copy-start.4
  12.8 9.8 %copy-start.8 = (s32[2,1]{0,1:T(1,128)S(1)}, s32[2,1]{0,1:T(1,128)}, u32[]{:S(2)}) copy-start(s32[2,1]{0,1:T(1,128)} %param.17) | copy-start | bytes 28
  16.8 12.8 %all-to-all-start = ((f32[4,1,13,128]{3,1,2,0:T(1,128)}), f32[4,1,13,128]{3,1,2,0:T(1,128)}, u32[]{:S(2)}, u32[]{:S(2)}) async-start(f32[4,1,13,128]{3,1,2,0:T(1,128)} %stack.28), calls=%async_computation | async-start | bytes 53248 | tf_op jit(solution)/shard_map/all_to_all | solution.py:14
  38.8 3.6 %copy-start.1 = (f32[400,20,1,128]{3,0,1,2:T(8,128)}, f32[400,20,1,128]{3,0,1,2:T(8,128)S(1)}, u32[]{:S(2)}) copy-start(f32[400,20,1,128]{3,0,1,2:T(8,128)S(1)} %convert_bitcast_fusion) | copy-start | bytes 12288004
  39.2 21.5 %collective-permute-start.1 = (bf16[200,2560]{1,0:T(8,128)(2,1)S(1)}, bf16[200,2560]{1,0:T(8,128)(2,1)}, u32[]{:S(2)}, u32[]{:S(2)}) collective-permute-start(bf16[200,2560]{1,0:T(8,128)(2,1)S(1)} %bitcast.73), channel_id=1, source_target_pairs={{0,4},{4,8},{8,12},{12,16},{16,20},{20,24},{24,28},{28,0},{1,5},{5... | collective-permute-start | bytes 3072008 | tf_op jit(solution)/shard_map/ppermute | solution.py:22
  42.4 3.9 %copy-start.7 = (f32[20]{0:T(128)S(1)}, f32[20]{0:T(128)}, u32[]{:S(2)}) copy-start(f32[20]{0:T(128)} %get-tuple-element.57) | copy-start | bytes 244
  42.4 23.1 %collective-permute-start = (bf16[200,2560]{1,0:T(8,128)(2,1)}, bf16[200,2560]{1,0:T(8,128)(2,1)}, u32[]{:S(2)}, u32[]{:S(2)}) collective-permute-start(bf16[200,2560]{1,0:T(8,128)(2,1)} %bitcast.71), channel_id=1, source_target_pairs={{0,28},{4,0},{8,4},{12,8},{16,12},{20,16},{24,20},{28,24},{1,29},{... | collective-permute-start | bytes 3072008 | tf_op jit(solution)/shard_map/ppermute | solution.py:22
  57.9 8.9 %copy-start.5 = (f32[400]{0:T(512)S(1)}, f32[400]{0:T(512)}, u32[]{:S(2)}) copy-start(f32[400]{0:T(512)} %get-tuple-element.48) | copy-start | bytes 4804
  57.9 8.9 %copy-start.6 = (f32[400]{0:T(512)S(1)}, f32[400]{0:T(512)}, u32[]{:S(2)}) copy-start(f32[400]{0:T(512)} %get-tuple-element.49) | copy-start | bytes 4804
  66.9 5.0 %copy-start.3 = (f32[400,20,1,1]{3,0,1,2:T(8,128)S(1)}, f32[400,20,1,1]{3,0,1,2:T(8,128)}, u32[]{:S(2)}) copy-start(f32[400,20,1,1]{3,0,1,2:T(8,128)} %copy.64) | copy-start | bytes 96004
  70.0 1.9 %copy-start.2 = (f32[400,20,1,128]{3,0,1,2:T(8,128)}, f32[400,20,1,128]{3,0,1,2:T(8,128)S(1)}, u32[]{:S(2)}) copy-start(f32[400,20,1,128]{3,0,1,2:T(8,128)S(1)} %fusion.4) | copy-start | bytes 12288004
